TPU v7x, 128 devices: a whole 4x4x4 slice. The times are simulated.
128 devices in a mesh: dp: 8 (over z, core), ts: 16 (over y, x).
Axes of the slice: x: 4, y: 4, z: 4, core: 2. Of those that a mesh axis runs over, the one named last changes fastest.
Arguments:
- text_embed: bfloat16 [8, 1024, 4096], P('dp', None, 'ts'), may hold values from -6 to 6
- bridge: bfloat16 [128, 32, 4096], P('dp', None, 'ts'), may hold values from -6 to 6
- crystal_slot: int32 [128], P('dp'), may hold values from 0 to 8159, as said below
- segments: int32 [8, 1024], P('dp'), may hold values from 0 to 15, as said below
- attn_gain: float32 [4096], replicated, may hold values from 0.1 to 1.9
- w_query: bfloat16 [4096, 4096], P(None, 'ts'), as said below
- w_key: bfloat16 [4096, 1024], P(None, 'ts'), may hold values from -0.09375 to 0.09375
- w_value: bfloat16 [4096, 1024], P(None, 'ts'), may hold values from -0.09375 to 0.09375
- w_out: bfloat16 [4096, 4096], P('ts'), may hold values from -0.09375 to 0.09375
- mlp_gain: float32 [4096], replicated, may hold values from 0.1 to 1.9
- w_gate: bfloat16 [4096, 12288], P(None, 'ts'), may hold values from -0.09375 to 0.09375
- w_up: bfloat16 [4096, 12288], P(None, 'ts'), may hold values from -0.09375 to 0.09375
- w_down: bfloat16 [12288, 4096], P('ts'), may hold values from -0.0546875 to 0.0546875
Outputs:
- layer_out: bfloat16 [8, 1024, 4096], P('dp', 'ts')
Inputs may be any that keep to these rules, and one draw needn't show every extreme that they name: `segments`: each row starts at 0, never falls and names every document number of 0 to 15; every document holds at least 33 positions. `crystal_slot`: each crystal's 32 rows take the first 32 positions of one document, given as sequence * 1024 + that document's first position; every document takes exactly one crystal, and each sequence takes exactly 2 of the 16 crystals held by each index of dp. `w_query`: entries lie within plus or minus 104 / sqrt(4096).
All inputs are finite; a program needn't handle non-finite values.
Results may differ from a plain program's by a relative error of at most 0.025.
The roundings to bfloat16 on the way count: a program that leaves them out, or rounds other values in their place, can miss the bound.
Values may be sent and summed in bfloat16 or wider, within the bound.
No kernel may reach another device: no remote copies, remote signals or barrier semaphores. Data moves between devices by JAX's collectives and lax.ppermute only.
A program may use at most 128 MiB of HBM per device.

v0:
```python
import jax
import jax.numpy as jnp
from jax import lax
from jax.sharding import PartitionSpec as P

HD = 128
DOC_LEN = 64
norm_epsilon = 1e-05
rope_base = 500000.0
masked_score = -1e30


def partner_2(block, axis, apart):
    count = lax.axis_size(axis)
    route = []
    for low in range(count):
        high = low | 1 << apart
        if high != low and high < count:
            route += [(low, high), (high, low)]
    return lax.ppermute(block, axis, route)


def norm_rows(rows, gain):
    widened = rows.astype(jnp.float32)
    inverse_rms = lax.rsqrt(jnp.mean(widened * widened, axis=-1, keepdims=True) + norm_epsilon)
    return (widened * inverse_rms * gain).astype(jnp.bfloat16)


def rotate_pairs(values, positions, first_pair):
    pair_count = values.shape[-1] // 2
    exponent = 2.0 * (first_pair + jnp.arange(pair_count, dtype=jnp.int32)).astype(jnp.float32) / HD
    frequency = rope_base ** (-exponent)
    angles = positions.astype(jnp.float32)[:, None] * frequency[None, :]
    cosine = jnp.cos(angles)[:, None, :]
    sine_part = jnp.sin(angles)[:, None, :]
    paired = values.reshape(values.shape[0], values.shape[1], pair_count, 2)
    even_part = paired[..., 0]
    odd_part = paired[..., 1]
    new_even = even_part * cosine - odd_part * sine_part
    new_odd = even_part * sine_part + odd_part * cosine
    return jnp.stack([new_even, new_odd], axis=-1).reshape(values.shape)


def attend_block(query_block, query_segments, query_index, keys_full, values_full, segment_ids):
    scores = jnp.einsum(
        "qhd,kd->hqk", query_block, keys_full, preferred_element_type=jnp.float32
    ) * HD ** (-0.5)
    key_index = jnp.arange(keys_full.shape[0], dtype=jnp.int32)
    allowed = (query_segments[:, None] == segment_ids[None, :]) & (
        key_index[None, :] <= query_index[:, None]
    )
    scores = jnp.where(allowed[None], scores, masked_score)
    row_top = jnp.max(scores, axis=-1, keepdims=True)
    weights = jnp.exp(scores - row_top)
    probabilities = (weights / jnp.sum(weights, axis=-1, keepdims=True)).astype(jnp.bfloat16)
    mixed_rows = jnp.einsum(
        "hqk,kd->qhd", probabilities, values_full, preferred_element_type=jnp.float32
    )
    return mixed_rows.astype(jnp.bfloat16).reshape(query_block.shape[0], -1)


def shards(
    text_embed,
    bridge,
    crystal_slot,
    segments,
    attn_gain,
    w_query,
    w_key,
    w_value,
    w_out,
    mlp_gain,
    w_gate,
    w_up,
    w_down,
):
    seq_len = text_embed.shape[1]
    part_width = text_embed.shape[2]
    doc_count = seq_len // DOC_LEN
    bridge_len = bridge.shape[1]
    tok_rows = seq_len // lax.axis_size("ts")
    group_index = lax.axis_index("dp")
    ts_index = lax.axis_index("ts")
    segment_ids = segments[0]
    doc_numbers = jnp.arange(doc_count, dtype=jnp.int32)
    starts = jnp.sum((segment_ids[None, :] < doc_numbers[:, None]).astype(jnp.int32), axis=1)
    doc_match = segment_ids[:, None] == doc_numbers[None, :]
    positions = jnp.arange(seq_len, dtype=jnp.int32) - jnp.sum(
        jnp.where(doc_match, starts[None, :], 0), axis=1
    )
    flat_bridge = bridge.reshape(bridge.shape[0], bridge_len * part_width)
    arrived, arrived_slots = (
        lax.all_gather(flat_bridge, "dp", axis=0, tiled=True),
        lax.all_gather(crystal_slot, "dp", axis=0, tiled=True),
    )
    wanted = group_index * seq_len + starts
    picking = wanted[:, None] == arrived_slots[None, :]
    by_doc = jnp.dot(
        picking.astype(jnp.bfloat16), arrived, preferred_element_type=jnp.float32
    ).astype(jnp.bfloat16)
    by_doc = by_doc.reshape(doc_count * bridge_len, part_width)
    in_bridge = positions < bridge_len
    row_pick = (segment_ids * bridge_len + positions)[:, None] == jnp.arange(
        doc_count * bridge_len, dtype=jnp.int32
    )[None, :]
    row_pick = row_pick & in_bridge[:, None]
    filled = jnp.dot(
        row_pick.astype(jnp.bfloat16), by_doc, preferred_element_type=jnp.float32
    ).astype(jnp.bfloat16)
    own_part = jnp.where(in_bridge[:, None], filled, text_embed[0])
    packed = lax.all_gather(own_part, "ts", axis=1, tiled=True)
    normed = norm_rows(packed, attn_gain)
    heads_here = w_query.shape[1] // HD
    queries = jnp.dot(normed, w_query, preferred_element_type=jnp.float32).reshape(
        seq_len, heads_here, HD
    )
    queries = rotate_pairs(queries, positions, 0).astype(jnp.bfloat16)
    kv_cols = w_key.shape[1]
    upper_half = ts_index % 2 == 1
    key_half = jnp.dot(normed, w_key, preferred_element_type=jnp.float32).reshape(
        seq_len, 1, kv_cols
    )
    key_half = rotate_pairs(key_half, positions, ts_index % 2 * (kv_cols // 2))
    key_half = key_half.astype(jnp.bfloat16).reshape(seq_len, kv_cols)
    value_half = jnp.dot(normed, w_value, preferred_element_type=jnp.float32).astype(jnp.bfloat16)
    own_pair = jnp.concatenate([key_half, value_half], axis=1)
    partner = partner_2(own_pair, "ts", 0)
    lower_half = jnp.where(upper_half, partner, own_pair)
    higher = jnp.where(upper_half, own_pair, partner)
    keys_full = jnp.concatenate([lower_half[:, :kv_cols], higher[:, :kv_cols]], axis=1)
    values_full = jnp.concatenate([lower_half[:, kv_cols:], higher[:, kv_cols:]], axis=1)
    block_rows = min(512, seq_len)
    outputs = []
    for block_index in range(seq_len // block_rows):
        first_row = block_index * block_rows
        query_index = jnp.arange(first_row, first_row + block_rows, dtype=jnp.int32)
        outputs.append(
            attend_block(
                queries[first_row : first_row + block_rows],
                segment_ids[first_row : first_row + block_rows],
                query_index,
                keys_full,
                values_full,
                segment_ids,
            )
        )
    attended = jnp.concatenate(outputs, axis=0)
    mine_offset = ts_index * tok_rows
    partial_rows = jnp.dot(attended, w_out, preferred_element_type=jnp.float32)
    attn_sum = lax.psum(partial_rows.astype(jnp.bfloat16), "ts").astype(jnp.float32)
    after_all = (packed.astype(jnp.float32) + attn_sum).astype(jnp.bfloat16)
    after_mine = lax.dynamic_slice_in_dim(after_all, mine_offset, tok_rows, 0)
    normed_mlp = norm_rows(after_all, mlp_gain)
    gate_proj = jnp.dot(normed_mlp, w_gate, preferred_element_type=jnp.float32)
    up_proj = jnp.dot(normed_mlp, w_up, preferred_element_type=jnp.float32)
    hidden = (jax.nn.silu(gate_proj) * up_proj).astype(jnp.bfloat16)
    mlp_mine = lax.psum_scatter(
        jnp.dot(hidden, w_down, preferred_element_type=jnp.float32).astype(jnp.bfloat16),
        "ts",
        scatter_dimension=0,
        tiled=True,
    ).astype(jnp.float32)
    layer_rows = (after_mine.astype(jnp.float32) + mlp_mine).astype(jnp.bfloat16)
    return layer_rows.reshape(1, tok_rows, layer_rows.shape[1])


def solution(mesh):
    return jax.shard_map(
        shards,
        mesh=mesh,
        in_specs=(
            P("dp", None, "ts"),
            P("dp", None, "ts"),
            P("dp"),
            P("dp", None),
            P(),
            P(None, "ts"),
            P(None, "ts"),
            P(None, "ts"),
            P("ts", None),
            P(),
            P(None, "ts"),
            P(None, "ts"),
            P("ts", None),
        ),
        out_specs=P("dp", "ts", None),
        check_vma=False,
    )
```

profile of v0, /device:TPU:0, one launch (start us, length us, event | category | flops | bytes accessed | tf_op | source)
XLA Modules:
  0.0 462.7 jit_solution(8637387790045024165)
XLA Ops:
  6.5 2.0 copy.65
  8.6 1.3 dynamic-slice
  11.4 10.6 %all-reduce = s32[128]{0:T(128)S(1)} all-reduce(s32[128]{0:T(128)S(1)} %dynamic-update-slice), channel_id=1, replica_groups=mesh['dp'=8,'ts'=16] {'dp'}, use_global_device_ids=true, to_apply=%add | all-reduce | flops 128 | bytes 1024
  24.3 12.6 %all-gather.3.cloned.1.call-done = bf16[128,8192]{1,0:T(8,128)(2,1)} async-done(((bf16[16,8192]{1,0:T(8,128)(2,1)}), bf16[128,8192]{1,0:T(8,128)(2,1)}) %all-gather.3.cloned.1.call-update) | async-done | bytes 2097168 | tf_op jit(solution)/shard_map/all_gather | solution.py:93
  37.0 2.0 convolution_convert_fusion
  39.1 2.7 fusion.36
  42.0 2.3 multiply_cosine_fusion
  44.3 1.6 fusion.22
  45.9 74.7 %all-gather.5.cloned.1.call-done = bf16[1024,4096]{1,0:T(8,128)(2,1)} async-done(((bf16[1024,256]{1,0:T(8,128)(2,1)}), bf16[1024,4096]{1,0:T(8,128)(2,1)}) %all-gather.5.cloned.1.call-update) | async-done | bytes 8388624 | tf_op jit(solution)/shard_map/all_gather | solution.py:111
  120.6 5.1 %fusion.5 = f32[1024]{0:T(1024)S(1)} fusion(bf16[1024,4096]{1,0:T(8,128)(2,1)} %all-gather.5.cloned.1.call-done), kind=kLoop, calls=%fused_computation.10 | loop fusion | flops 12581888 | bytes 8392704 | tf_op jit(solution)/shard_map/reduce_sum | solution.py:25
  125.7 10.4 %fusion.7 = bf16[1024,4096]{1,0:T(8,128)(2,1)} fusion(bf16[1024,4096]{1,0:T(8,128)(2,1)} %all-gather.5.cloned.1.call-done, f32[4096]{0:T(1024)S(1)} %copy-done.8, f32[1024]{0:T(1024)S(1)} %add_rsqrt_fusion.1), kind=kLoop, calls=%fused_computation.12 | loop fusion | flops 16777216 | bytes 16797696 | tf_op jit(solution)/shard_map/convert_element_type | solution.py:26
  136.1 6.2 %convolution_convert_fusion.3 = bf16[1024,64]{0,1:T(8,128)(2,1)S(1)} fusion(bf16[1024,4096]{1,0:T(8,128)(2,1)} %fusion.7, bf16[4096,64]{0,1:T(8,128)(2,1)S(1)} %copy-done.4), kind=kOutput, calls=%fused_computation.48 | convolution fusion | flops 536936448 | bytes 9043968 | tf_op jit(solution)/shard_map/dot_general | solution.py:125
  142.4 2.7 fusion.103
  145.0 3.6 fusion.104
  148.7 1.8 reshape_reshape.7
  150.5 0.9 reshape_reshape.6
  151.4 1.3 fusion.91
  154.3 1.3 collective-permute-start
  155.5 2.1 subtract_convert_fusion
  157.6 1.2 fusion.51
  158.9 2.7 collective-permute-done
  161.7 4.8 %fusion.98 = (f32[2,512]{1,0:T(2,128)S(1)}, f32[2,512,1024]{1,2,0:T(8,128)}) fusion(pred[512,1024]{0,1:T(8,128)(4,1)} %get-tuple-element.25, bf16[512,2,128]{0,1,2:T(2,128)(2,1)} %bitcast.86, bf16[1024,64]{0,1:T(8,128)(2,1)S(1)} %get-tuple-element.35, bf16[1024,64]{0,1:T(8,128)(2,1)S(1)} %get-tuple-element.18), kind=kOutput, calls=%fused_computation.119 | convolution fusion | flops 273155072 | bytes 5246976 | tf_op jit(solution)/shard_map/sub | solution.py:54
  166.5 3.7 fusion.93
  170.2 2.8 fusion.40
  174.2 5.6 %convolution_convert_fusion.2 = bf16[1024,4096]{1,0:T(8,128)(2,1)} fusion(bf16[256,4096]{1,0:T(8,128)(2,1)S(1)} %copy-done, bf16[512,256]{0,1:T(8,128)(2,1)S(1)} %bitcast.83, bf16[512,256]{0,1:T(8,128)(2,1)S(1)} %bitcast.82), kind=kOutput, calls=%fused_computation.16 | convolution fusion | flops 2152726528 | bytes 11010048 | tf_op jit(solution)/shard_map/dot_general | solution.py:149
  179.8 140.8 %all-reduce.3.cloned.1.call-done = bf16[1024,4096]{1,0:T(8,128)(2,1)} async-done(((bf16[1024,4096]{1,0:T(8,128)(2,1)}), bf16[1024,4096]{1,0:T(8,128)(2,1)}) %all-reduce.3.cloned.1.call-update) | async-done | bytes 8388624 | tf_op jit(solution)/shard_map/psum | solution.py:150
  320.6 8.0 %fusion.2 = (f32[1024]{0:T(1024)S(1)}, bf16[1024,4096]{1,0:T(8,128)(2,1)S(1)}) fusion(bf16[1024,4096]{1,0:T(8,128)(2,1)} %all-reduce.3.cloned.1.call-done, bf16[1024,4096]{1,0:T(8,128)(2,1)} %all-gather.5.cloned.1.call-done), kind=kLoop, calls=%fused_computation.7 | loop fusion | flops 29359104 | bytes 25169920 | tf_op jit(solution)/shard_map/reduce_sum | solution.py:25
  328.7 3.2 copy-done.3
  331.9 11.3 %fusion.11 = f32[1024,768]{1,0:T(8,128)} fusion(bf16[4096,768]{1,0:T(8,128)(2,1)} %param.24, bf16[1024,4096]{1,0:T(8,128)(2,1)S(1)} %get-tuple-element.6, f32[4096]{0:T(1024)S(1)} %copy-done.10, f32[1024]{0:T(1024)S(1)} %add_rsqrt_fusion), kind=kOutput, calls=%fused_computation.26 | convolution fusion | flops 6459228160 | bytes 17846272 | tf_op jit(solution)/shard_map/dot_general | solution.py:155
  343.2 26.4 %convolution_convert_fusion.1 = bf16[1024,4096]{1,0:T(8,128)(2,1)} fusion(bf16[768,4096]{1,0:T(8,128)(2,1)} %param.25, f32[1024,768]{1,0:T(8,128)} %fusion.11, bf16[4096,768]{1,0:T(8,128)(2,1)} %param.23, bf16[1024,4096]{1,0:T(8,128)(2,1)} %copy-done.3, f32[4096]{0:T(1024)S(1)} %copy-done.10, f32[1024]{0:T(1024)S(1)} %add_rsqrt_fusion), kind=kOutput, calls=%fused_computation.15 | convolution fusion | flops 12910592000 | bytes 32526336 | tf_op jit(solution)/shard_map/dot_general | solution.py:158
  369.6 84.2 %reduce-scatter.2.cloned.1.call-done = bf16[64,4096]{1,0:T(8,128)(2,1)} async-done(((bf16[1024,4096]{1,0:T(8,128)(2,1)}), bf16[64,4096]{1,0:T(8,128)(2,1)}) %reduce-scatter.2.cloned.1.call-update) | async-done | bytes 524304 | tf_op jit(solution)/shard_map/reduce_scatter | solution.py:157
  453.8 2.1 fusion.43
  (54 shorter events, 6.5 us)
Async XLA Ops:
  6.5 167.6 %copy-start = (bf16[256,4096]{1,0:T(8,128)(2,1)S(1)}, bf16[256,4096]{1,0:T(8,128)(2,1)}, u32[]{:S(2)}) copy-start(bf16[256,4096]{1,0:T(8,128)(2,1)} %param.21) | copy-start | bytes 6291460
  6.5 35.4 %copy-start.7 = (s32[1,1024]{1,0:T(1,128)S(1)}, s32[1,1024]{1,0:T(1,128)}, u32[]{:S(2)}) copy-start(s32[1,1024]{1,0:T(1,128)} %param.16) | copy-start | bytes 12292
  6.5 30.4 %all-gather.3.cloned.1.call-start = ((), (), s32[]{:S(2)}) async-start(), calls=%async_computation.1 | async-start | bytes 2359296 | tf_op jit(solution)/shard_map/all_gather | solution.py:93
  8.5 112.1 %all-gather.5.cloned.1.call-start = ((), (), s32[]{:S(2)}) async-start(), calls=%async_computation.2 | async-start | bytes 8912896 | tf_op jit(solution)/shard_map/all_gather | solution.py:111
  39.1 86.6 %copy-start.8 = (f32[4096]{0:T(1024)S(1)}, f32[4096]{0:T(1024)}, u32[]{:S(2)}) copy-start(f32[4096]{0:T(1024)} %param.17) | copy-start | bytes 49156
  41.9 278.8 %all-reduce.3.cloned.1.call-start = ((), (), s32[]{:S(2)}) async-start(), calls=%async_computation.3 | async-start | bytes 16777216 | tf_op jit(solution)/shard_map/psum | solution.py:150
  125.7 10.4 %copy-start.4 = (bf16[4096,64]{0,1:T(8,128)(2,1)S(1)}, bf16[4096,64]{0,1:T(8,128)(2,1)}, u32[]{:S(2)}) copy-start(bf16[4096,64]{0,1:T(8,128)(2,1)} %param.20) | copy-start | bytes 1572868
  136.1 6.2 %copy-start.2 = (bf16[1024,4096]{1,0:T(8,128)(2,1)S(1)}, bf16[1024,4096]{1,0:T(8,128)(2,1)}, u32[]{:S(2)}) copy-start(bf16[1024,4096]{1,0:T(8,128)(2,1)} %fusion.7) | copy-start | bytes 25165828
  136.1 6.2 %copy-start.5 = (bf16[4096,64]{0,1:T(8,128)(2,1)S(1)}, bf16[4096,64]{0,1:T(8,128)(2,1)}, u32[]{:S(2)}) copy-start(bf16[4096,64]{0,1:T(8,128)(2,1)} %param.19) | copy-start | bytes 1572868
  142.3 2.7 copy-start.9
  154.3 7.3 %collective-permute-start = (bf16[1024,128]{0,1:T(8,128)(2,1)S(1)}, bf16[1024,128]{0,1:T(8,128)(2,1)S(1)}, u32[]{:S(2)}, u32[]{:S(2)}) collective-permute-start(bf16[1024,128]{0,1:T(8,128)(2,1)S(1)} %pad_maximum_fusion.1), channel_id=1, source_target_pairs={{0,1},{1,0},{2,3},{3,2},{4,5},{5,4},{6,7},{7,6},{8,9},{9,8},{10,11... | collective-permute-start | bytes 786440 | tf_op jit(solution)/shard_map/ppermute | solution.py:20
  157.6 8.9 %copy-start.6 = (pred[512,1024]{0,1:T(8,128)(4,1)S(1)}, pred[512,1024]{0,1:T(8,128)(4,1)}, u32[]{:S(2)}) copy-start(pred[512,1024]{0,1:T(8,128)(4,1)} %get-tuple-element.26) | copy-start | bytes 1572868
  170.2 3.4 copy-start.11
  179.8 152.1 %copy-start.10 = (f32[4096]{0:T(1024)S(1)}, f32[4096]{0:T(1024)}, u32[]{:S(2)}) copy-start(f32[4096]{0:T(1024)} %param.22) | copy-start | bytes 49156
  179.8 274.0 %reduce-scatter.2.cloned.1.call-start = ((), (), s32[]{:S(2)}) async-start(), calls=%async_computation.4 | async-start | bytes 8912896 | tf_op jit(solution)/shard_map/reduce_scatter | solution.py:157
  328.7 3.2 copy-start.3
  343.2 112.7 %copy-start.1 = (bf16[256,4096]{1,0:T(8,128)(2,1)S(1)}, bf16[256,4096]{1,0:T(8,128)(2,1)}, u32[]{:S(2)}) copy-start(bf16[256,4096]{1,0:T(8,128)(2,1)} %param.21) | copy-start | bytes 6291460
Sparse Core Ops, SparseCore 0:
  9.1 27.8 all-gather.2
  42.0 78.5 all-gather.4
  179.9 140.6 all-reduce.2
  369.7 84.0 reduce-scatter.1
where the time goes:
time: 466 us; the launch traced here: 463 us
  waiting for transfers between devices  315 us (68%)
  matrix products  72.3 us (16%)
  other arithmetic  35.9 us (8%)
  between operations  14.3 us (3%)
  local copies, waits for them, and re-layouts  13.2 us (3%)
  blocking collectives  10.6 us (2%)
    psum x1, waiting for transfers between devices, shards(): lax.psum(partial_rows.astype(jnp.bfloat16), 'ts').astype(jnp.float32)  141 us
    reduce_scatter x1, waiting for transfers between devices, shards(): lax.psum_scatter(jnp.dot(hidden, w_down, preferred_element_type=jnp.float...  84.2 us
    all_gather x1, waiting for transfers between devices, shards(): packed = lax.all_gather(own_part, 'ts', axis=1, tiled=True)  74.7 us
    dot_general x1, matrix products, shards(): jnp.dot(hidden, w_down, preferred_element_type=jnp.float32)  26.4 us
    reduce_sum x2, other arithmetic, norm_rows(): jnp.mean(widened * widened, axis=-1, keepdims=True) + norm_epsilon  13.1 us
    all_gather x1, waiting for transfers between devices, shards(): lax.all_gather(flat_bridge, 'dp', axis=0, tiled=True)  12.6 us
    dot_general x1, matrix products, shards(): up_proj = jnp.dot(normed_mlp, w_up, preferred_element_type=jnp.float32)  11.3 us
    unnamed x1, blocking collectives  10.6 us
  transfers between devices with their start and end apart: 5, of which 5 were waited for; matrix products, arithmetic and copies ran while one was open for 3% of the time, Pallas kernels for 0%

commit v1 on v0

--- a/solution.py
+++ b/solution.py
@@ -108,7 +108,10 @@
         row_pick.astype(jnp.bfloat16), by_doc, preferred_element_type=jnp.float32
     ).astype(jnp.bfloat16)
     own_part = jnp.where(in_bridge[:, None], filled, text_embed[0])
-    packed = lax.all_gather(own_part, "ts", axis=1, tiled=True)
+    choose_shelves = lambda point: jnp.concatenate(
+        lax.all_to_all(jnp.stack([point] * lax.axis_size("ts")), "ts", 0, 0), 1
+    )
+    packed = choose_shelves(own_part)
     normed = norm_rows(packed, attn_gain)
     heads_here = w_query.shape[1] // HD
     queries = jnp.dot(normed, w_query, preferred_element_type=jnp.float32).reshape(

time: 466 us -> 558 us (1.20)
  local copies, waits for them, and re-layouts: 13.2 us -> 56.4 us
  waiting for transfers between devices: 315 us -> 353 us
  starting transfers between devices: 1.38 us -> 8.01 us
    all_to_all x0 -> x1, waiting for transfers between devices: none -> 114 us  [shards(): lax.all_to_all(jnp.stack([point] * lax.axis_size('ts')), 'ts', 0, 0)]
    all_gather x1 -> x0, waiting for transfers between devices: 74.7 us -> none  [shards(): packed = lax.all_gather(own_part, 'ts', axis=1, tiled=True)]
    convert_element_type x0 -> x1, local copies, waits for them, and re-layouts: none -> 17.5 us  [shards(): after_all = (packed.astype(jnp.float32) + attn_sum).astype(jnp.bfloat16)]
    all_to_all x0 -> x1, local copies, waits for them, and re-layouts: none -> 12.3 us  [shards(): lax.all_to_all(jnp.stack([point] * lax.axis_size('ts')), 'ts', 0, 0)]
    dot_general x0 -> x2, local copies, waits for them, and re-layouts: none -> 8.61 us  [shards(): jnp.dot(normed, w_query, preferred_element_type=jnp.float32)]
    all_to_all x0 -> x1, starting transfers between devices: none -> 6.99 us  [shards(): lax.all_to_all(jnp.stack([point] * lax.axis_size('ts')), 'ts', 0, 0)]
    unnamed x28 -> x34, local copies, waits for them, and re-layouts: 8.03 us -> 11.2 us
  transfers between devices with their start and end apart: 5 -> 5, of which waited for: 5 -> 5; matrix products, arithmetic and copies ran while one was open for 3% -> 4% of each run, Pallas kernels for 0% -> 0%
where the time goes in v1:
time: 558 us; the launch traced here: 554 us
  waiting for transfers between devices  353 us (63%)
  matrix products  73 us (13%)
  local copies, waits for them, and re-layouts  56.4 us (10%)
  other arithmetic  38.7 us (7%)
  between operations  14.4 us (3%)
  blocking collectives  10.6 us (2%)
  starting transfers between devices  8.01 us (1%)
    psum x1, waiting for transfers between devices, shards(): lax.psum(partial_rows.astype(jnp.bfloat16), 'ts').astype(jnp.float32)  139 us
    all_to_all x1, waiting for transfers between devices, shards(): lax.all_to_all(jnp.stack([point] * lax.axis_size('ts')), 'ts', 0, 0)  114 us
    reduce_scatter x1, waiting for transfers between devices, shards(): lax.psum_scatter(jnp.dot(hidden, w_down, preferred_element_type=jnp.float...  84.1 us
    dot_general x1, matrix products, shards(): jnp.dot(hidden, w_down, preferred_element_type=jnp.float32)  26.4 us
    convert_element_type x1, local copies, waits for them, and re-layouts, shards(): after_all = (packed.astype(jnp.float32) + attn_sum).astype(jnp.bfloat16)  17.5 us
    reduce_sum x2, other arithmetic, norm_rows(): jnp.mean(widened * widened, axis=-1, keepdims=True) + norm_epsilon  14.5 us
    all_gather x1, waiting for transfers between devices, shards(): lax.all_gather(flat_bridge, 'dp', axis=0, tiled=True)  12.7 us
    all_to_all x1, local copies, waits for them, and re-layouts, shards(): lax.all_to_all(jnp.stack([point] * lax.axis_size('ts')), 'ts', 0, 0)  12.3 us
  transfers between devices with their start and end apart: 5, of which 5 were waited for; matrix products, arithmetic and copies ran while one was open for 4% of the time, Pallas kernels for 0%

profile of v1, /device:TPU:0, one launch (start us, length us, event | category | flops | bytes accessed | tf_op | source)
XLA Modules:
  0.0 553.8 jit_solution(3626922174794946746)
XLA Ops:
  6.5 1.9 copy.88
  11.4 10.6 %all-reduce = s32[128]{0:T(128)S(1)} all-reduce(s32[128]{0:T(128)S(1)} %dynamic-update-slice), channel_id=1, replica_groups=mesh['dp'=8,'ts'=16] {'dp'}, use_global_device_ids=true, to_apply=%add | all-reduce | flops 128 | bytes 1024
  24.3 12.7 %all-gather.2.cloned.1.call-done = bf16[128,8192]{1,0:T(8,128)(2,1)} async-done(((bf16[16,8192]{1,0:T(8,128)(2,1)}), bf16[128,8192]{1,0:T(8,128)(2,1)}) %all-gather.2.cloned.1.call-update) | async-done | bytes 2097168 | tf_op jit(solution)/shard_map/all_gather | solution.py:93
  37.0 2.0 convolution_convert_fusion
  39.1 2.0 fusion.37
  41.1 4.0 stack.8
  45.2 7.0 %all-to-all-start = ((bf16[16,1024,256]{2,1,0:T(8,128)(2,1)}), bf16[16,1024,256]{2,1,0:T(8,128)(2,1)}, u32[]{:S(2)}, u32[]{:S(2)}) async-start(bf16[16,1024,256]{2,1,0:T(8,128)(2,1)} %stack.8), calls=%async_computation | async-start | bytes 16777216 | tf_op jit(solution)/shard_map/all_to_all | solution.py:112
  53.1 4.2 copy.66
  57.3 4.4 dot_general.54
  62.7 1.7 fusion.23
  64.4 113.6 %all-to-all-done = bf16[16,1024,256]{2,1,0:T(8,128)(2,1)} async-done(((bf16[16,1024,256]{2,1,0:T(8,128)(2,1)}), bf16[16,1024,256]{2,1,0:T(8,128)(2,1)}, u32[]{:S(2)}, u32[]{:S(2)}) %all-to-all-start) | async-done | bytes 8388640 | tf_op jit(solution)/shard_map/all_to_all | solution.py:112
  178.0 12.3 %copy.61 = bf16[16,1024,256]{1,2,0:T(8,128)(2,1)} copy(bf16[16,1024,256]{2,1,0:T(8,128)(2,1)} %all-to-all-done) | data formatting | bytes 16777216 | tf_op jit(solution)/shard_map/all_to_all | solution.py:112
  190.3 5.1 multiply_reduce_fusion
  195.4 11.3 %convert_element_type.147 = f32[16,1024,256]{1,2,0:T(8,128)} convert(bf16[16,1024,256]{1,2,0:T(8,128)(2,1)} %copy.61) | non-fusion elementwise | flops 4194304 | bytes 25165824 | tf_op jit(solution)/shard_map/convert_element_type | solution.py:154
  206.7 5.0 multiply_convert_fusion.1
  211.7 3.2 copy-done.3
  214.9 1.6 convolution_bitcast_fusion
  217.3 17.5 %copy.83 = f32[1024,4096]{1,0:T(8,128)} copy(f32[1024,4096]{0,1:T(8,128)} %bitcast.88) | data formatting | bytes 33554432 | tf_op jit(solution)/shard_map/convert_element_type | solution.py:154
  234.8 8.6 %fusion.42 = bf16[1024,64]{0,1:T(8,128)(2,1)S(1)} fusion(bf16[4096,64]{0,1:T(8,128)(2,1)S(1)} %copy-done.6, f32[1024,4096]{1,0:T(8,128)} %copy.83, f32[4096]{0:T(1024)S(1)} %copy-done.10, f32[1024]{0:T(1024)S(1)} %add_rsqrt_fusion.1), kind=kOutput, calls=%fused_computation.51 | convolution fusion | flops 549519360 | bytes 17453056 | tf_op jit(solution)/shard_map/dot_general | solution.py:128
  243.8 2.7 fusion.14
  248.0 3.1 collective-permute-done
  252.0 4.8 fusion.98
  256.8 4.7 fusion.93
  261.5 2.8 fusion.41
  265.4 5.6 %convolution_convert_fusion.2 = bf16[1024,4096]{1,0:T(8,128)(2,1)} fusion(bf16[256,4096]{1,0:T(8,128)(2,1)S(1)} %copy-done, bf16[512,256]{0,1:T(8,128)(2,1)S(1)} %bitcast.95, bf16[512,256]{0,1:T(8,128)(2,1)S(1)} %bitcast.94), kind=kOutput, calls=%fused_computation.16 | convolution fusion | flops 2152726528 | bytes 11010048 | tf_op jit(solution)/shard_map/dot_general | solution.py:152
  271.3 139.2 %all-reduce.3.cloned.1.call-done = bf16[1024,4096]{1,0:T(8,128)(2,1)} async-done(((bf16[1024,4096]{1,0:T(8,128)(2,1)}), bf16[1024,4096]{1,0:T(8,128)(2,1)}) %all-reduce.3.cloned.1.call-update) | async-done | bytes 8388624 | tf_op jit(solution)/shard_map/psum | solution.py:153
  410.5 9.4 %fusion.2 = (f32[1024]{0:T(1024)S(1)}, bf16[1024,4096]{1,0:T(8,128)(2,1)S(1)}) fusion(f32[1024,4096]{1,0:T(8,128)} %copy.83, bf16[1024,4096]{1,0:T(8,128)(2,1)} %all-reduce.3.cloned.1.call-done), kind=kLoop, calls=%fused_computation.4 | loop fusion | flops 25164800 | bytes 33558528 | tf_op jit(solution)/shard_map/reduce_sum | solution.py:25
  419.9 3.2 copy-done.2
  423.1 11.3 %fusion.10 = f32[1024,768]{1,0:T(8,128)} fusion(bf16[4096,768]{1,0:T(8,128)(2,1)} %param.24, bf16[1024,4096]{1,0:T(8,128)(2,1)S(1)} %get-tuple-element.6, f32[4096]{0:T(1024)S(1)} %copy-done.13, f32[1024]{0:T(1024)S(1)} %add_rsqrt_fusion), kind=kOutput, calls=%fused_computation.26 | convolution fusion | flops 6459228160 | bytes 17846272 | tf_op jit(solution)/shard_map/dot_general | solution.py:158
  434.4 26.4 %convolution_convert_fusion.1 = bf16[1024,4096]{1,0:T(8,128)(2,1)} fusion(bf16[768,4096]{1,0:T(8,128)(2,1)} %param.25, f32[1024,768]{1,0:T(8,128)} %fusion.10, bf16[4096,768]{1,0:T(8,128)(2,1)} %param.23, bf16[1024,4096]{1,0:T(8,128)(2,1)} %copy-done.2, f32[4096]{0:T(1024)S(1)} %copy-done.13, f32[1024]{0:T(1024)S(1)} %add_rsqrt_fusion), kind=kOutput, calls=%fused_computation.15 | convolution fusion | flops 12910592000 | bytes 32526336 | tf_op jit(solution)/shard_map/dot_general | solution.py:161
  460.8 84.1 %reduce-scatter.2.cloned.1.call-done = bf16[64,4096]{1,0:T(8,128)(2,1)} async-done(((bf16[1024,4096]{1,0:T(8,128)(2,1)}), bf16[64,4096]{1,0:T(8,128)(2,1)}) %reduce-scatter.2.cloned.1.call-update) | async-done | bytes 524304 | tf_op jit(solution)/shard_map/reduce_scatter | solution.py:160
  544.9 2.1 fusion.45
  (65 shorter events, 11.4 us)
Async XLA Ops:
  6.5 258.9 %copy-start = (bf16[256,4096]{1,0:T(8,128)(2,1)S(1)}, bf16[256,4096]{1,0:T(8,128)(2,1)}, u32[]{:S(2)}) copy-start(bf16[256,4096]{1,0:T(8,128)(2,1)} %param.21) | copy-start | bytes 6291460
  6.5 30.4 %all-gather.2.cloned.1.call-start = ((), (), s32[]{:S(2)}) async-start(), calls=%async_computation.2 | async-start | bytes 2359296 | tf_op jit(solution)/shard_map/all_gather | solution.py:93
  45.2 7.5 %copy-start.10 = (f32[4096]{0:T(1024)S(1)}, f32[4096]{0:T(1024)}, u32[]{:S(2)}) copy-start(f32[4096]{0:T(1024)} %param.17) | copy-start | bytes 49156
  45.2 7.6 %copy-start.7 = (bf16[4096,64]{0,1:T(8,128)(2,1)S(1)}, bf16[4096,64]{0,1:T(8,128)(2,1)}, u32[]{:S(2)}) copy-start(bf16[4096,64]{0,1:T(8,128)(2,1)} %param.19) | copy-start | bytes 1572868
  45.2 132.8 %all-to-all-start = ((bf16[16,1024,256]{2,1,0:T(8,128)(2,1)}), bf16[16,1024,256]{2,1,0:T(8,128)(2,1)}, u32[]{:S(2)}, u32[]{:S(2)}) async-start(bf16[16,1024,256]{2,1,0:T(8,128)(2,1)} %stack.8), calls=%async_computation | async-start | bytes 16777216 | tf_op jit(solution)/shard_map/all_to_all | solution.py:112
  52.2 9.6 %copy-start.12 = (s32[1,1024]{1,0:T(1,128)S(1)}, s32[1,1024]{1,0:T(1,128)}, u32[]{:S(2)}) copy-start(s32[1,1024]{1,0:T(1,128)} %param.16) | copy-start | bytes 12292
  52.2 358.3 %all-reduce.3.cloned.1.call-start = ((), (), s32[]{:S(2)}) async-start(), calls=%async_computation.3 | async-start | bytes 16777216 | tf_op jit(solution)/shard_map/psum | solution.py:153
  211.7 3.2 copy-start.3
  217.3 17.5 %copy-start.6 = (bf16[4096,64]{0,1:T(8,128)(2,1)S(1)}, bf16[4096,64]{0,1:T(8,128)(2,1)}, u32[]{:S(2)}) copy-start(bf16[4096,64]{0,1:T(8,128)(2,1)} %param.20) | copy-start | bytes 1572868
  234.8 8.9 %copy-start.4 = (bf16[16,1024,256]{1,2,0:T(8,128)(2,1)S(1)}, bf16[16,1024,256]{1,2,0:T(8,128)(2,1)}, u32[]{:S(2)}) copy-start(bf16[16,1024,256]{1,2,0:T(8,128)(2,1)} %copy-done.3) | copy-start | bytes 25165828
  234.8 9.0 %copy-start.5 = (bf16[2,64,2,4096]{3,2,1,0:T(2,128)(2,1)S(1)}, bf16[2,64,2,4096]{3,2,1,0:T(2,128)(2,1)}, u32[]{:S(2)}) copy-start(bf16[2,64,2,4096]{3,2,1,0:T(2,128)(2,1)} %dot_general.54) | copy-start | bytes 6291460
  243.5 7.6 %collective-permute-start = (bf16[1024,128]{0,1:T(8,128)(2,1)S(1)}, bf16[1024,128]{0,1:T(8,128)(2,1)S(1)}, u32[]{:S(2)}, u32[]{:S(2)}) collective-permute-start(bf16[1024,128]{0,1:T(8,128)(2,1)S(1)} %pad_maximum_fusion.1), channel_id=1, source_target_pairs={{0,1},{1,0},{2,3},{3,2},{4,5},{5,4},{6,7},{7,6},{8,9},{9,8},{10,11... | collective-permute-start | bytes 786440 | tf_op jit(solution)/shard_map/ppermute | solution.py:20
  246.5 5.5 copy-start.9
  246.7 10.1 %copy-start.8 = (pred[512,1024]{0,1:T(8,128)(4,1)S(1)}, pred[512,1024]{0,1:T(8,128)(4,1)}, u32[]{:S(2)}) copy-start(pred[512,1024]{0,1:T(8,128)(4,1)} %get-tuple-element.22) | copy-start | bytes 1572868
  256.8 4.7 copy-start.11
  261.5 3.4 copy-start.14
  271.1 152.0 %copy-start.13 = (f32[4096]{0:T(1024)S(1)}, f32[4096]{0:T(1024)}, u32[]{:S(2)}) copy-start(f32[4096]{0:T(1024)} %param.22) | copy-start | bytes 49156
  271.1 273.9 %reduce-scatter.2.cloned.1.call-start = ((), (), s32[]{:S(2)}) async-start(), calls=%async_computation.4 | async-start | bytes 8912896 | tf_op jit(solution)/shard_map/reduce_scatter | solution.py:160
  419.9 3.2 copy-start.2
  434.4 112.7 %copy-start.1 = (bf16[256,4096]{1,0:T(8,128)(2,1)S(1)}, bf16[256,4096]{1,0:T(8,128)(2,1)}, u32[]{:S(2)}) copy-start(bf16[256,4096]{1,0:T(8,128)(2,1)} %param.21) | copy-start | bytes 6291460
Sparse Core Ops, SparseCore 0:
  9.1 27.8 all-gather.1
  271.2 139.2 all-reduce.2
  460.9 83.9 reduce-scatter.1
